TPU v7x, 32 devices: a whole 2x2x4 slice. The times are simulated.
32 devices in a mesh: seq: 8 (over z, x), tp: 4 (over y, core).
Axes of the slice: x: 2, y: 2, z: 4, core: 2. Of those that a mesh axis runs over, the one named last changes fastest.
Arguments:
- queries: bfloat16 [1024, 4096], P('seq', 'tp'), may hold values from -600 to 600
- suffix_keys: bfloat16 [1024, 1024], P('seq', 'tp'), may hold values from -6 to 6
- suffix_values: bfloat16 [1024, 1024], P('seq', 'tp'), may hold values from -6 to 6
- prefix_keys: bfloat16 [512, 1024], P('seq', 'tp'), may hold values from -6 to 6
- prefix_values: bfloat16 [512, 1024], P('seq', 'tp'), may hold values from -6 to 6
- suffix_lengths: int32 [24], replicated, may hold values from 1 to 128, 1024 in all
- request_group: int32 [24], replicated, may hold values from 0 to 3
- block_group: int32 [8], replicated, may hold values from 0 to 3, as said below
Outputs:
- attended: bfloat16 [1024, 4096], P('seq', 'tp')
- cache_keys: bfloat16 [1024, 1024], P(('seq', 'tp'))
- cache_values: bfloat16 [1024, 1024], P(('seq', 'tp'))
Inputs may be any that keep to these rules, and one draw needn't show every extreme that they name: `suffix_lengths`: the suffixes fill the 1024 packed tokens end to end in order; the longest has exactly 128 tokens. `block_group`: each prefix is held by exactly 2 blocks, in any order.
All inputs are finite; a program needn't handle non-finite values.
Results may differ from a plain program's by a relative error of at most 0.009.
The roundings to bfloat16 on the way count: a program that leaves them out, or rounds other values in their place, can miss the bound.
Values may be sent and summed in bfloat16 or wider, within the bound.
No kernel may reach another device: no remote copies, remote signals or barrier semaphores. Data moves between devices by JAX's collectives and lax.ppermute only.
A program may use at most 64 MiB of HBM per device.

v0:
```python
import math
import jax
import jax.numpy as jnp
from jax import lax
from jax.sharding import PartitionSpec as P

HD = 128
GROUPS = 4
BIG_NEGATIVE = -1e30


def from_behind(array, axis, by):
    length = lax.axis_size(axis)
    pairs = [(i, i + by) for i in range(length) if 0 <= i + by < length]
    return lax.ppermute(array, axis, pairs)


def rotate(values, position):
    half = values.shape[-1] // 2
    freq = jnp.exp(
        jnp.arange(half, dtype=jnp.float32) * (-2.0 * math.log(500000.0) / values.shape[-1])
    )
    angle = position.astype(jnp.float32)[:, None] * freq[None, :]
    cosine = jnp.cos(angle)[:, None, :]
    sine = jnp.sin(angle)[:, None, :]
    floats = values.astype(jnp.float32)
    lower = floats[..., :half]
    upper = floats[..., half:]
    return jnp.concatenate(
        [lower * cosine - upper * sine, upper * cosine + lower * sine], axis=-1
    ).astype(jnp.bfloat16)


def token_info(index, suffix_lengths, request_group):
    ends = jnp.cumsum(suffix_lengths)
    request = jnp.sum((index[:, None] >= ends[None, :]).astype(jnp.int32), axis=1)
    onehot = request[:, None] == jnp.arange(suffix_lengths.shape[0], dtype=jnp.int32)[None, :]
    first = jnp.sum(jnp.where(onehot, (ends - suffix_lengths)[None, :], 0), axis=1)
    group = jnp.sum(jnp.where(onehot, request_group[None, :], 0), axis=1)
    return (request, index - first, group)


def body(
    queries,
    suffix_keys,
    suffix_values,
    prefix_keys,
    prefix_values,
    suffix_lengths,
    request_group,
    block_group,
):
    rows = queries.shape[0]
    kv_cols = suffix_keys.shape[1]
    kv_heads = kv_cols // HD
    q_heads = queries.shape[1] // HD
    repeat = q_heads // kv_heads
    devices = lax.axis_size("seq")
    me = lax.axis_index("seq")
    block_rows = prefix_keys.shape[0]
    prefix_len = block_rows * devices // GROUPS
    span = max(1, min(2048 // rows, devices // 8))
    scale = HD ** (-0.5)
    index = me * rows + jnp.arange(rows, dtype=jnp.int32)
    request, offset, group = token_info(index, suffix_lengths, request_group)
    position = offset + prefix_len
    q_rot = rotate(queries.reshape(rows, q_heads, HD), position).reshape(rows, kv_heads, repeat, HD)
    k_rot = rotate(suffix_keys.reshape(rows, kv_heads, HD), position).reshape(rows, kv_cols)

    def update(carry, keys, values, visible):
        high, total, accum = carry
        keys_split = keys.reshape(keys.shape[0], kv_heads, HD)
        values_split = values.reshape(values.shape[0], kv_heads, HD)
        scores = (
            jnp.einsum("bgrd,kgd->bgrk", q_rot, keys_split, preferred_element_type=jnp.float32)
            * scale
        )
        mask = visible[:, None, None, :]
        scores = jnp.where(mask, scores, BIG_NEGATIVE)
        new_high = jnp.maximum(high, jnp.max(scores, axis=-1))
        weights = jnp.where(mask, jnp.exp(scores - new_high[..., None]), 0.0)
        factor = jnp.exp(high - new_high)
        total = total * factor + jnp.sum(weights, axis=-1)
        accum = accum * factor[..., None] + jnp.einsum(
            "bgrk,kgd->bgrd",
            weights.astype(jnp.bfloat16),
            values_split,
            preferred_element_type=jnp.float32,
        )
        return (new_high, total, accum)

    def guarded(carry, keys, values, visible):
        return update(carry, keys, values, visible)

    def suffix_visible(back):
        key_index = (me - back) * rows + jnp.arange(rows, dtype=jnp.int32)
        key_request, _, _ = token_info(key_index, suffix_lengths, request_group)
        return (
            (key_index[None, :] >= 0)
            & (key_request[None, :] == request[:, None])
            & (key_index[None, :] <= index[:, None])
        )

    start_state = (
        jnp.full((rows, kv_heads, repeat), BIG_NEGATIVE, jnp.float32),
        jnp.zeros((rows, kv_heads, repeat), jnp.float32),
        jnp.zeros((rows, kv_heads, repeat, HD), jnp.float32),
    )
    carry = start_state
    keys = lax.all_gather(prefix_keys, "seq", axis=0, tiled=True)
    values = lax.all_gather(prefix_values, "seq", axis=0, tiled=True)
    count = keys.shape[0]
    width = 512

    def one_step(state, step):
        first = step * width
        keys_part = lax.dynamic_slice_in_dim(keys, first, width, 0)
        values_part = lax.dynamic_slice_in_dim(values, first, width, 0)
        row_index = first + jnp.arange(width, dtype=jnp.int32)
        holder = row_index // block_rows
        matches = holder[:, None] == jnp.arange(block_group.shape[0], dtype=jnp.int32)[None, :]
        row_group = jnp.sum(jnp.where(matches, block_group[None, :], 0), axis=1)
        visible = row_group[None, :] == group[:, None]
        return (guarded(state, keys_part, values_part, visible), None)

    carry, _ = lax.scan(one_step, carry, jnp.arange(count // width, dtype=jnp.int32))
    carry = guarded(carry, k_rot, suffix_values, suffix_visible(0))
    for back in range(1, span + 1):
        earlier_keys, earlier_values = from_behind((k_rot, suffix_values), "seq", back)
        carry = guarded(carry, earlier_keys, earlier_values, suffix_visible(back))
    high, total, accum = carry
    attended = (accum / total[..., None]).reshape(rows, q_heads * HD).astype(jnp.bfloat16)
    cache_keys, cache_values = (
        lax.all_to_all(k_rot, "tp", split_axis=0, concat_axis=1, tiled=True),
        lax.all_to_all(suffix_values, "tp", split_axis=0, concat_axis=1, tiled=True),
    )
    return (attended, cache_keys, cache_values)


def solution(mesh):
    return jax.shard_map(
        body,
        mesh=mesh,
        in_specs=(
            P("seq", "tp"),
            P("seq", "tp"),
            P("seq", "tp"),
            P("seq", "tp"),
            P("seq", "tp"),
            P(),
            P(),
            P(),
        ),
        out_specs=(P("seq", "tp"), P(("seq", "tp"), None), P(("seq", "tp"), None)),
        check_vma=False,
    )
```

profile of v0, /device:TPU:0, one launch (start us, length us, event | category | flops | bytes accessed | tf_op | source)
XLA Modules:
  0.0 101.6 jit_solution(3033059807300362979)
XLA Ops:
  0.7 0.8 copy.95
  2.4 0.7 select_reduce_fusion.2
  3.1 0.9 copy.101
  4.7 0.7 copy.106
  5.5 5.5 %collective-permute-start = (bf16[128,256]{0,1:T(8,128)(2,1)}, bf16[128,256]{0,1:T(8,128)(2,1)}, u32[]{:S(2)}, u32[]{:S(2)}) collective-permute-start(bf16[128,256]{0,1:T(8,128)(2,1)} %bitcast.19), channel_id=1, source_target_pairs={{0,4},{4,8},{8,12},{12,16},{16,20},{20,24},{24,28},{1,5},{5,9},{9,... | collective-permute-start | bytes 196616 | tf_op jit(solution)/shard_map/ppermute | solution.py:15
  10.9 3.5 %collective-permute-start.1 = (bf16[128,256]{1,0:T(8,128)(2,1)}, bf16[128,256]{1,0:T(8,128)(2,1)}, u32[]{:S(2)}, u32[]{:S(2)}) collective-permute-start(bf16[128,256]{1,0:T(8,128)(2,1)} %param.10), channel_id=1, source_target_pairs={{0,4},{4,8},{8,12},{12,16},{16,20},{20,24},{24,28},{1,5},{5,9},{9,... | collective-permute-start | bytes 196616 | tf_op jit(solution)/shard_map/ppermute | solution.py:15
  15.2 3.3 %all-to-all-start = ((bf16[4,32,256]{2,1,0:T(8,128)(2,1)}), bf16[4,32,256]{2,1,0:T(8,128)(2,1)S(1)}, u32[]{:S(2)}, u32[]{:S(2)}) async-start(bf16[4,32,256]{2,1,0:T(8,128)(2,1)} %convert_element_type.70), calls=%async_computation | async-start | bytes 131072 | tf_op jit(solution)/shard_map/all_to_all | solution.py:134
  18.9 31.0 %all_gather.6 = bf16[512,256]{1,0:T(8,128)(2,1)S(1)} all-gather(bf16[64,256]{1,0:T(8,128)(2,1)S(1)} %copy-done.7), channel_id=1, replica_groups=mesh['seq'=8,'tp'=4] {'seq'}, dimensions={0}, use_global_device_ids=true | all-gather | bytes 294912 | tf_op jit(solution)/shard_map/all_gather | solution.py:110
  50.4 0.8 compare_and_fusion
  51.2 1.2 %bitcast_reduce_fusion = (f32[128,2,4]{0,2,1:T(4,128)}, f32[2,128,4,512]{3,1,2,0:T(8,128)S(1)}) fusion(pred[128,512]{1,0:T(8,128)(4,1)S(1)} %broadcast_compare_fusion, bf16[512,2,128,1]{0,2,3,1:T(8,128)(2,1)S(1)} %bitcast.101, bf16[128,2,4,64]{3,0,2,1:T(8,128)(2,1)S(1)} %bitcast.98, bf16[128,2,4,64]{3,0,2,1:T(8,128)(2,1)S(1)} %bitcast.95), kind=kOutput, calls=%fused_computation.1 | convolution fusion | flops 136313856 | bytes 2691072 | tf_op jit(solution)/shard_map/while/body/eval_jaxpr/bgrd,kgd->bgrk/dot_general | solution.py:75
  52.4 0.9 fusion.49
  53.9 3.9 %all-to-all-start.1 = ((bf16[4,32,256]{2,1,0:T(8,128)(2,1)}), bf16[4,32,256]{2,1,0:T(8,128)(2,1)}, u32[]{:S(2)}, u32[]{:S(2)}) async-start(bf16[4,32,256]{2,1,0:T(8,128)(2,1)} %bitcast.29), calls=%async_computation.1 | async-start | bytes 131072 | tf_op jit(solution)/shard_map/all_to_all | solution.py:135
  57.8 31.0 %all_gather.7 = bf16[512,256]{1,0:T(8,128)(2,1)S(1)} all-gather(bf16[64,256]{1,0:T(8,128)(2,1)} %param.12), channel_id=1, replica_groups=mesh['seq'=8,'tp'=4] {'seq'}, dimensions={0}, use_global_device_ids=true | all-gather | bytes 294912 | tf_op jit(solution)/shard_map/all_gather | solution.py:111
  88.9 0.9 copy.124
  89.8 0.8 copy.100
  90.7 1.5 %copy.131 = bf16[4,4,8,256]{3,2,0,1:T(8,128)(2,1)} copy(bf16[4,4,8,256]{3,2,1,0:T(8,128)(2,1)} %bitcast.106) | data formatting | bytes 131072 | tf_op jit(solution)/shard_map/all_to_all | solution.py:134
  92.2 1.5 %copy.132 = bf16[4,4,8,256]{3,2,0,1:T(8,128)(2,1)} copy(bf16[4,4,8,256]{3,2,1,0:T(8,128)(2,1)} %bitcast.46) | data formatting | bytes 131072 | tf_op jit(solution)/shard_map/all_to_all | solution.py:135
  93.6 1.2 %fusion.48 = (f32[128,2,4]{0,2,1:T(4,128)S(1)}, f32[128,2,4,128]{0,3,2,1:T(8,128)S(1)}) fusion(bf16[128,2,128,1]{0,2,3,1:T(8,128)(2,1)} %bitcast.39, bf16[128,2,4,64]{3,0,2,1:T(8,128)(2,1)S(1)} %bitcast.100, bf16[128,2,4,64]{3,0,2,1:T(8,128)(2,1)S(1)} %bitcast.97, pred[128,128]{0,1:T(8,128)(4,1)} %get-tuple-element.67), kind=kOutput, calls=%fused_computation.88 | convolution fusion | flops 34470912 | bytes 872448 | tf_op jit(solution)/shard_map/bgrd,kgd->bgrk/dot_general | solution.py:75
  94.9 0.7 fusion.44
  96.0 0.7 fusion.2
  96.9 1.6 %fusion.7 = f32[128,2,4,128]{0,3,2,1:T(8,128)} fusion(f32[128,2,4,128]{0,3,2,1:T(8,128)S(1)} %convolution_bitcast_fusion.1, bf16[512,2,128,1]{0,2,3,1:T(8,128)(2,1)S(1)} %bitcast.104, f32[2,128,4,512]{3,1,2,0:T(8,128)S(1)} %get-tuple-element.76, f32[128,2,4]{0,2,1:T(4,128)S(1)} %get-tuple-element.66, pred[128,512]{1,0:T(8,128)(4,1)S(1)} %broadcast_compare_fusion, ...), kind=kOutput, calls=%fused_computation.13 | convolution fusion | flops 137363456 | bytes 3489792 | tf_op jit(solution)/shard_map/while/body/eval_jaxpr/bgrk,kgd->bgrd/dot_general | solution.py:84
  98.5 0.9 copy.108
  99.4 1.3 %fusion.14 = bf16[128,2,4,128]{0,3,2,1:T(8,128)(2,1)S(1)} fusion(f32[128,2,4,128]{0,3,2,1:T(8,128)} %fusion.7, bf16[128,2,128,1]{0,2,3,1:T(8,128)(2,1)S(1)} %bitcast.109, f32[128,2,4,128]{0,3,2,1:T(8,128)S(1)} %copy-done.1, f32[128,2,4]{0,2,1:T(4,128)S(1)} %get-tuple-element.52, f32[128,2,4]{0,2,1:T(4,128)S(1)} %get-tuple-element.55, ...), kind=kOutput, calls=%fused_computation.22 | convolution fusion | flops 34340864 | bytes 1400832 | tf_op jit(solution)/shard_map/bgrk,kgd->bgrd/dot_general | solution.py:84
  100.7 0.9 copy.113
  (50 shorter events, 4.4 us)
Async XLA Ops:
  0.6 17.9 %copy-start.2 = (bf16[128,1024]{1,0:T(8,128)(2,1)S(1)}, bf16[128,1024]{1,0:T(8,128)(2,1)}, u32[]{:S(2)}) copy-start(bf16[128,1024]{1,0:T(8,128)(2,1)} %param.8) | copy-start | bytes 786436
  5.5 88.2 %collective-permute-start = (bf16[128,256]{0,1:T(8,128)(2,1)}, bf16[128,256]{0,1:T(8,128)(2,1)}, u32[]{:S(2)}, u32[]{:S(2)}) collective-permute-start(bf16[128,256]{0,1:T(8,128)(2,1)} %bitcast.19), channel_id=1, source_target_pairs={{0,4},{4,8},{8,12},{12,16},{16,20},{20,24},{24,28},{1,5},{5,9},{9,... | collective-permute-start | bytes 196616 | tf_op jit(solution)/shard_map/ppermute | solution.py:15
  10.9 87.5 %collective-permute-start.1 = (bf16[128,256]{1,0:T(8,128)(2,1)}, bf16[128,256]{1,0:T(8,128)(2,1)}, u32[]{:S(2)}, u32[]{:S(2)}) collective-permute-start(bf16[128,256]{1,0:T(8,128)(2,1)} %param.10), channel_id=1, source_target_pairs={{0,4},{4,8},{8,12},{12,16},{16,20},{20,24},{24,28},{1,5},{5,9},{9,... | collective-permute-start | bytes 196616 | tf_op jit(solution)/shard_map/ppermute | solution.py:15
  14.5 4.4 %copy-start.7 = (bf16[64,256]{1,0:T(8,128)(2,1)S(1)}, bf16[64,256]{1,0:T(8,128)(2,1)}, u32[]{:S(2)}) copy-start(bf16[64,256]{1,0:T(8,128)(2,1)} %param.11) | copy-start | bytes 98308
  15.2 38.1 %all-to-all-start = ((bf16[4,32,256]{2,1,0:T(8,128)(2,1)}), bf16[4,32,256]{2,1,0:T(8,128)(2,1)S(1)}, u32[]{:S(2)}, u32[]{:S(2)}) async-start(bf16[4,32,256]{2,1,0:T(8,128)(2,1)} %convert_element_type.70), calls=%async_computation | async-start | bytes 131072 | tf_op jit(solution)/shard_map/all_to_all | solution.py:134
  18.6 31.6 %copy-start.8 = (s32[8]{0:T(128)S(1)}, s32[8]{0:T(128)}, u32[]{:S(2)}) copy-start(s32[8]{0:T(128)} %param.15) | copy-start | bytes 100
  53.3 0.6 copy-start.4
  53.9 38.2 %all-to-all-start.1 = ((bf16[4,32,256]{2,1,0:T(8,128)(2,1)}), bf16[4,32,256]{2,1,0:T(8,128)(2,1)}, u32[]{:S(2)}, u32[]{:S(2)}) async-start(bf16[4,32,256]{2,1,0:T(8,128)(2,1)} %bitcast.29), calls=%async_computation.1 | async-start | bytes 131072 | tf_op jit(solution)/shard_map/all_to_all | solution.py:135
  94.9 2.0 %copy-start = (f32[128,2,4,128]{0,3,2,1:T(8,128)}, f32[128,2,4,128]{0,3,2,1:T(8,128)S(1)}, u32[]{:S(2)}) copy-start(f32[128,2,4,128]{0,3,2,1:T(8,128)S(1)} %get-tuple-element.72) | copy-start | bytes 1572868
  94.9 1.8 %copy-start.5 = (pred[128,128]{0,1:T(8,128)(4,1)S(1)}, pred[128,128]{0,1:T(8,128)(4,1)}, u32[]{:S(2)}) copy-start(pred[128,128]{0,1:T(8,128)(4,1)} %get-tuple-element.67) | copy-start | bytes 49156
  95.7 1.1 %copy-start.6 = (f32[128,2,4]{0,2,1:T(4,128)S(1)}, f32[128,2,4]{0,2,1:T(4,128)}, u32[]{:S(2)}) copy-start(f32[128,2,4]{0,2,1:T(4,128)} %get-tuple-element.75) | copy-start | bytes 12292
  95.7 1.1 %copy-start.3 = (bf16[512,256]{0,1:T(8,128)(2,1)S(1)}, bf16[512,256]{0,1:T(8,128)(2,1)}, u32[]{:S(2)}) copy-start(bf16[512,256]{0,1:T(8,128)(2,1)} %copy.100) | copy-start | bytes 786436
  96.9 2.6 %copy-start.1 = (f32[128,2,4,128]{0,3,2,1:T(8,128)S(1)}, f32[128,2,4,128]{0,3,2,1:T(8,128)}, u32[]{:S(2)}) copy-start(f32[128,2,4,128]{0,3,2,1:T(8,128)} %copy-done) | copy-start | bytes 1572868
where the time goes:
time: 102 us
  blocking collectives  62 us (61%)
  starting transfers between devices  16.1 us (16%)
  local copies, waits for them, and re-layouts  11.1 us (11%)
  matrix products  6.46 us (6%)
  other arithmetic  5.01 us (5%)
    all_gather x1, blocking collectives, body(): values = lax.all_gather(prefix_values, 'seq', axis=0, tiled=True)  31 us
    all_gather x1, blocking collectives, body(): keys = lax.all_gather(prefix_keys, 'seq', axis=0, tiled=True)  31 us
    ppermute x2, starting transfers between devices, from_behind(): return lax.ppermute(array, axis, pairs)  8.92 us
    all_to_all x1, starting transfers between devices, body(): lax.all_to_all(suffix_values, 'tp', split_axis=0, concat_axis=1, tiled=True)  3.89 us
    dot_general x3, matrix products, update(): jnp.einsum('bgrd,kgd->bgrk', q_rot, keys_split, preferred_element_type=jn...  3.34 us
    all_to_all x1, starting transfers between devices, body(): lax.all_to_all(k_rot, 'tp', split_axis=0, concat_axis=1, tiled=True)  3.28 us
    dot_general x3, matrix products, update(): jnp.einsum('bgrk,kgd->bgrd', weights.astype(jnp.bfloat16), values_split,...  3.12 us
    unnamed x23, local copies, waits for them, and re-layouts  2.76 us
  transfers between devices with their start and end apart: 4, of which 0 were waited for; matrix products, arithmetic and copies ran while one was open for 14% of the time, Pallas kernels for 0%

commit v1 on v0

--- a/solution.py
+++ b/solution.py
@@ -7,6 +7,19 @@
 HD = 128
 GROUPS = 4
 BIG_NEGATIVE = -1e30
+
+
+def ring_gather(array, axis, dim):
+    ways = lax.axis_size(axis)
+    up = [(d, (d + 1) % ways) for d in range(ways)]
+    down = [(d, (d - 1) % ways) for d in range(ways)]
+    earlier, later = ([array], [array])
+    for _ in range(ways // 2):
+        earlier.append(lax.ppermute(earlier[-1], axis, up))
+    for _ in range((ways - 1) // 2):
+        later.append(lax.ppermute(later[-1], axis, down))
+    line = jnp.concatenate([*earlier[::-1], *later[1:]], axis=dim)
+    return jnp.roll(line, (lax.axis_index(axis) - ways // 2) * array.shape[dim], axis=dim)
 
 
 def from_behind(array, axis, by):
@@ -108,7 +121,7 @@
     )
     carry = start_state
     keys = lax.all_gather(prefix_keys, "seq", axis=0, tiled=True)
-    values = lax.all_gather(prefix_values, "seq", axis=0, tiled=True)
+    values = ring_gather(prefix_values, "seq", 0)
     count = keys.shape[0]
     width = 512
 

time: 102 us -> 95.2 us (0.933)
  blocking collectives: 62 us -> 31.2 us
  starting transfers between devices: 16.1 us -> 28 us
  waiting for transfers between devices: 0.01 us -> 8.52 us
  local copies, waits for them, and re-layouts: 11.1 us -> 14.2 us
    all_gather x1 -> x0, blocking collectives: 31 us -> none  [body(): values = lax.all_gather(prefix_values, 'seq', axis=0, tiled=True)]
    ppermute x0 -> x7, starting transfers between devices: none -> 15.7 us  [the longest x3 12.6 us: ring_gather(): later.append(lax.ppermute(later[-1], axis, down))]
    ppermute x0 -> x7, waiting for transfers between devices: none -> 8.51 us  [the longest x4 8.5 us: ring_gather(): earlier.append(lax.ppermute(earlier[-1], axis, up))]
    unnamed x23 -> x36, local copies, waits for them, and re-layouts: 2.76 us -> 8.53 us
    ppermute x2, starting transfers between devices: 8.92 us -> 5.8 us  [from_behind(): return lax.ppermute(array, axis, pairs)]
    dot_general x3, matrix products: 3.34 us -> 2.31 us  [update(): jnp.einsum('bgrd,kgd->bgrk', q_rot, keys_split, preferred_element_type=jn...]
  transfers between devices with their start and end apart: 4 -> 11, of which waited for: 0 -> 2; matrix products, arithmetic and copies ran while one was open for 14% -> 20% of each run, Pallas kernels for 0% -> 0%
where the time goes in v1:
time: 95.2 us; the launch traced here: 94.1 us
  blocking collectives  31.2 us (33%)
  starting transfers between devices  28 us (29%)
  local copies, waits for them, and re-layouts  14.2 us (15%)
  waiting for transfers between devices  8.52 us (9%)
  matrix products  6.27 us (7%)
  other arithmetic  4.87 us (5%)
  between operations  0.98 us (1%)
    all_gather x1, blocking collectives, body(): keys = lax.all_gather(prefix_keys, 'seq', axis=0, tiled=True)  31.2 us
    ppermute x3, starting transfers between devices, ring_gather(): later.append(lax.ppermute(later[-1], axis, down))  12.6 us
    unnamed x36, local copies, waits for them, and re-layouts  8.53 us
    ppermute x4, waiting for transfers between devices, ring_gather(): earlier.append(lax.ppermute(earlier[-1], axis, up))  8.5 us
    ppermute x2, starting transfers between devices, from_behind(): return lax.ppermute(array, axis, pairs)  5.8 us
    dot_general x3, matrix products, update(): jnp.einsum('bgrk,kgd->bgrd', weights.astype(jnp.bfloat16), values_split,...  3.96 us
    all_to_all x1, starting transfers between devices, body(): lax.all_to_all(k_rot, 'tp', split_axis=0, concat_axis=1, tiled=True)  3.29 us
    all_to_all x1, starting transfers between devices, body(): lax.all_to_all(suffix_values, 'tp', split_axis=0, concat_axis=1, tiled=True)  3.29 us
  transfers between devices with their start and end apart: 11, of which 2 were waited for; matrix products, arithmetic and copies ran while one was open for 20% of the time, Pallas kernels for 0%

profile of v1, /device:TPU:0, one launch (start us, length us, event | category | flops | bytes accessed | tf_op | source)
XLA Modules:
  0.0 94.1 jit_solution(5587068092609812729)
XLA Ops:
  0.6 3.0 %collective-permute-start = (bf16[64,256]{1,0:T(8,128)(2,1)}, bf16[64,256]{1,0:T(8,128)(2,1)}, u32[]{:S(2)}, u32[]{:S(2)}) collective-permute-start(bf16[64,256]{1,0:T(8,128)(2,1)} %param.12), channel_id=1, source_target_pairs={{0,4},{4,8},{8,12},{12,16},{16,20},{20,24},{24,28},{28,0},{1,5},{5... | collective-permute-start | bytes 98312 | tf_op jit(solution)/shard_map/ppermute | solution.py:18
  3.6 3.1 %collective-permute-start.4 = (bf16[64,256]{1,0:T(8,128)(2,1)}, bf16[64,256]{1,0:T(8,128)(2,1)}, u32[]{:S(2)}, u32[]{:S(2)}) collective-permute-start(bf16[64,256]{1,0:T(8,128)(2,1)} %param.12), channel_id=1, source_target_pairs={{0,28},{4,0},{8,4},{12,8},{16,12},{20,16},{24,20},{28,24},{1,29},{... | collective-permute-start | bytes 98312 | tf_op jit(solution)/shard_map/ppermute | solution.py:20
  6.7 1.9 %collective-permute-start.8 = (bf16[128,256]{1,0:T(8,128)(2,1)}, bf16[128,256]{1,0:T(8,128)(2,1)}, u32[]{:S(2)}, u32[]{:S(2)}) collective-permute-start(bf16[128,256]{1,0:T(8,128)(2,1)} %param.10), channel_id=1, source_target_pairs={{0,4},{4,8},{8,12},{12,16},{16,20},{20,24},{24,28},{1,5},{5,9},{9,... | collective-permute-start | bytes 196616 | tf_op jit(solution)/shard_map/ppermute | solution.py:28
  8.6 3.3 %all-to-all-start.1 = ((bf16[4,32,256]{2,1,0:T(8,128)(2,1)}), bf16[4,32,256]{2,1,0:T(8,128)(2,1)S(1)}, u32[]{:S(2)}, u32[]{:S(2)}) async-start(bf16[4,32,256]{2,1,0:T(8,128)(2,1)} %bitcast.107), calls=%async_computation.1 | async-start | bytes 131072 | tf_op jit(solution)/shard_map/all_to_all | solution.py:148
  14.4 0.9 %copy.101 = bf16[128,256]{0,1:T(8,128)(2,1)S(1)} copy(bf16[128,256]{1,0:T(8,128)(2,1)} %param.9) | data formatting | bytes 131072 | tf_op args[1]
  16.7 3.9 %collective-permute-start.7 = (bf16[128,256]{0,1:T(8,128)(2,1)}, bf16[128,256]{0,1:T(8,128)(2,1)}, u32[]{:S(2)}, u32[]{:S(2)}) collective-permute-start(bf16[128,256]{0,1:T(8,128)(2,1)} %bitcast.19), channel_id=1, source_target_pairs={{0,4},{4,8},{8,12},{12,16},{16,20},{20,24},{24,28},{1,5},{5,9},{9,... | collective-permute-start | bytes 196616 | tf_op jit(solution)/shard_map/ppermute | solution.py:28
  20.6 31.2 %all_gather.3 = bf16[512,256]{1,0:T(8,128)(2,1)S(1)} all-gather(bf16[64,256]{1,0:T(8,128)(2,1)} %param.11), channel_id=1, replica_groups=mesh['seq'=8,'tp'=4] {'seq'}, dimensions={0}, use_global_device_ids=true | all-gather | bytes 294912 | tf_op jit(solution)/shard_map/all_gather | solution.py:123
  54.7 3.3 %all-to-all-start = ((bf16[4,32,256]{2,1,0:T(8,128)(2,1)}), bf16[4,32,256]{2,1,0:T(8,128)(2,1)S(1)}, u32[]{:S(2)}, u32[]{:S(2)}) async-start(bf16[4,32,256]{2,1,0:T(8,128)(2,1)} %convert_element_type.70), calls=%async_computation | async-start | bytes 131072 | tf_op jit(solution)/shard_map/all_to_all | solution.py:147
  59.1 4.7 %collective-permute-start.5 = (bf16[64,256]{1,0:T(8,128)(2,1)}, bf16[64,256]{1,0:T(8,128)(2,1)}, u32[]{:S(2)}, u32[]{:S(2)}) collective-permute-start(bf16[64,256]{1,0:T(8,128)(2,1)} %collective-permute-done.4), channel_id=1, source_target_pairs={{0,28},{4,0},{8,4},{12,8},{16,12},{20,16},{24,20},{28,24},{1,29},{... | collective-permute-start | bytes 98312 | tf_op jit(solution)/shard_map/ppermute | solution.py:20
  65.1 1.3 %fusion.48 = (f32[128,2,4]{0,2,1:T(4,128)S(1)}, f32[128,2,4,128]{0,3,2,1:T(8,128)S(1)}) fusion(bf16[128,2,128,1]{0,2,3,1:T(8,128)(2,1)} %bitcast.39, bf16[128,2,4,64]{3,0,2,1:T(8,128)(2,1)} %bitcast.100, bf16[128,2,4,64]{3,0,2,1:T(8,128)(2,1)S(1)} %bitcast.97, pred[128,128]{0,1:T(8,128)(4,1)S(1)} %get-tuple-element.68), kind=kOutput, calls=%fused_computation.105 | convolution fusion | flops 34470912 | bytes 872448 | tf_op jit(solution)/shard_map/bgrd,kgd->bgrk/dot_general | solution.py:88
  67.1 1.3 %fusion.2 = f32[128,2,4]{0,2,1:T(4,128)} fusion(f32[2,128,4,512]{3,1,2,0:T(8,128)S(1)} %get-tuple-element.76, f32[128,2,4]{0,2,1:T(4,128)S(1)} %get-tuple-element.66, pred[128,512]{1,0:T(8,128)(4,1)S(1)} %broadcast_compare_fusion), kind=kLoop, calls=%fused_computation.5 | loop fusion | flops 2620416 | bytes 2170880 | tf_op jit(solution)/shard_map/while/body/eval_jaxpr/reduce_sum | solution.py:96
  68.4 1.0 %copy.108 = bf16[128,256]{0,1:T(8,128)(2,1)S(1)} copy(bf16[128,256]{1,0:T(8,128)(2,1)} %collective-permute-done.8) | data formatting | bytes 131072 | tf_op jit(solution)/shard_map/ppermute | solution.py:28
  69.3 1.0 %convolution_bitcast_fusion = f32[128,2,4,128]{0,3,2,1:T(8,128)} fusion(bf16[128,2,128,1]{0,2,3,1:T(8,128)(2,1)S(1)} %bitcast.104, f32[128,2,4,128]{0,3,2,1:T(8,128)S(1)} %get-tuple-element.72, f32[128,2,4]{0,2,1:T(4,128)S(1)} %get-tuple-element.55, pred[128,128]{0,1:T(8,128)(4,1)S(1)} %get-tuple-element.68), kind=kOutput, calls=%fused_computation.7 | convolution fusion | flops 33947648 | bytes 1134592 | tf_op jit(solution)/shard_map/bgrk,kgd->bgrd/dot_general | solution.py:97
  70.4 1.1 %convolution_bitcast_fusion.1 = f32[128,2,4,128]{0,3,2,1:T(8,128)} fusion(bf16[128,2,128,1]{0,2,3,1:T(8,128)(2,1)S(1)} %bitcast.103, f32[128,2,4,128]{0,3,2,1:T(8,128)S(1)} %get-tuple-element.74, f32[128,2,4]{0,2,1:T(4,128)S(1)} %get-tuple-element.56, pred[128,128]{0,1:T(8,128)(4,1)S(1)} %get-tuple-element.67), kind=kOutput, calls=%fused_computation.8 | convolution fusion | flops 33947648 | bytes 1134592 | tf_op jit(solution)/shard_map/bgrk,kgd->bgrd/dot_general | solution.py:97
  71.7 6.7 %collective-permute-done.2 = bf16[64,256]{1,0:T(8,128)(2,1)S(1)} collective-permute-done((bf16[64,256]{1,0:T(8,128)(2,1)}, bf16[64,256]{1,0:T(8,128)(2,1)S(1)}, u32[]{:S(2)}, u32[]{:S(2)}) %collective-permute-start.2) | collective-permute-done | bytes 32800 | tf_op jit(solution)/shard_map/ppermute | solution.py:18
  78.5 4.8 %collective-permute-start.6 = (bf16[64,256]{1,0:T(8,128)(2,1)}, bf16[64,256]{1,0:T(8,128)(2,1)S(1)}, u32[]{:S(2)}, u32[]{:S(2)}) collective-permute-start(bf16[64,256]{1,0:T(8,128)(2,1)} %collective-permute-done.5), channel_id=1, source_target_pairs={{0,28},{4,0},{8,4},{12,8},{16,12},{20,16},{24,20},{28,24},{1,29},{... | collective-permute-start | bytes 98312 | tf_op jit(solution)/shard_map/ppermute | solution.py:20
  83.2 1.8 %collective-permute-done.3 = bf16[64,256]{1,0:T(8,128)(2,1)S(1)} collective-permute-done((bf16[64,256]{1,0:T(8,128)(2,1)S(1)}, bf16[64,256]{1,0:T(8,128)(2,1)S(1)}, u32[]{:S(2)}, u32[]{:S(2)}) %collective-permute-start.3) | collective-permute-done | bytes 32800 | tf_op jit(solution)/shard_map/ppermute | solution.py:18
  85.1 0.8 constant_dynamic-update-slice_fusion.13
  85.8 0.8 constant_dynamic-update-slice_fusion.12
  86.6 0.8 constant_dynamic-update-slice_fusion.10
  87.3 0.8 constant_dynamic-update-slice_fusion.9
  88.1 0.8 constant_dynamic-update-slice_fusion.5
  91.4 1.9 %fusion.14 = bf16[128,2,4,128]{0,3,2,1:T(8,128)(2,1)S(1)} fusion(f32[128,2,4,128]{0,3,2,1:T(8,128)} %convolution_bitcast_fusion, f32[128,2,4,128]{0,3,2,1:T(8,128)S(1)} %copy-done.1, bf16[512,2,128,1]{0,2,3,1:T(8,128)(2,1)S(1)} %bitcast.105, f32[2,128,4,512]{3,1,2,0:T(8,128)S(1)} %get-tuple-element.76, f32[128,2,4]{0,2,1:T(4,128)S(1)} %get-tuple-element.66, ...), kind=kOutput, calls=%fused_computation.22 | convolution fusion | flops 137756672 | bytes 3756032 | tf_op jit(solution)/shard_map/while/body/eval_jaxpr/bgrk,kgd->bgrd/dot_general | solution.py:97
  93.3 0.9 copy.113
  (78 shorter events, 12.3 us)
Async XLA Ops:
  0.6 51.4 %copy-start.2 = (bf16[128,1024]{1,0:T(8,128)(2,1)S(1)}, bf16[128,1024]{1,0:T(8,128)(2,1)}, u32[]{:S(2)}) copy-start(bf16[128,1024]{1,0:T(8,128)(2,1)} %param.8) | copy-start | bytes 786436
  0.6 58.5 %collective-permute-start = (bf16[64,256]{1,0:T(8,128)(2,1)}, bf16[64,256]{1,0:T(8,128)(2,1)}, u32[]{:S(2)}, u32[]{:S(2)}) collective-permute-start(bf16[64,256]{1,0:T(8,128)(2,1)} %param.12), channel_id=1, source_target_pairs={{0,4},{4,8},{8,12},{12,16},{16,20},{20,24},{24,28},{28,0},{1,5},{5... | collective-permute-start | bytes 98312 | tf_op jit(solution)/shard_map/ppermute | solution.py:18
  3.6 55.5 %collective-permute-start.4 = (bf16[64,256]{1,0:T(8,128)(2,1)}, bf16[64,256]{1,0:T(8,128)(2,1)}, u32[]{:S(2)}, u32[]{:S(2)}) collective-permute-start(bf16[64,256]{1,0:T(8,128)(2,1)} %param.12), channel_id=1, source_target_pairs={{0,28},{4,0},{8,4},{12,8},{16,12},{20,16},{24,20},{28,24},{1,29},{... | collective-permute-start | bytes 98312 | tf_op jit(solution)/shard_map/ppermute | solution.py:20
  6.7 61.6 %collective-permute-start.8 = (bf16[128,256]{1,0:T(8,128)(2,1)}, bf16[128,256]{1,0:T(8,128)(2,1)}, u32[]{:S(2)}, u32[]{:S(2)}) collective-permute-start(bf16[128,256]{1,0:T(8,128)(2,1)} %param.10), channel_id=1, source_target_pairs={{0,4},{4,8},{8,12},{12,16},{16,20},{20,24},{24,28},{1,5},{5,9},{9,... | collective-permute-start | bytes 196616 | tf_op jit(solution)/shard_map/ppermute | solution.py:28
  8.6 46.1 %all-to-all-start.1 = ((bf16[4,32,256]{2,1,0:T(8,128)(2,1)}), bf16[4,32,256]{2,1,0:T(8,128)(2,1)S(1)}, u32[]{:S(2)}, u32[]{:S(2)}) async-start(bf16[4,32,256]{2,1,0:T(8,128)(2,1)} %bitcast.107), calls=%async_computation.1 | async-start | bytes 131072 | tf_op jit(solution)/shard_map/all_to_all | solution.py:148
  16.7 48.4 %collective-permute-start.7 = (bf16[128,256]{0,1:T(8,128)(2,1)}, bf16[128,256]{0,1:T(8,128)(2,1)}, u32[]{:S(2)}, u32[]{:S(2)}) collective-permute-start(bf16[128,256]{0,1:T(8,128)(2,1)} %bitcast.19), channel_id=1, source_target_pairs={{0,4},{4,8},{8,12},{12,16},{16,20},{20,24},{24,28},{1,5},{5,9},{9,... | collective-permute-start | bytes 196616 | tf_op jit(solution)/shard_map/ppermute | solution.py:28
  52.0 0.7 copy-start.7
  53.1 5.2 %copy-start = (bf16[128,8,64]{2,0,1:T(8,128)(2,1)}, bf16[128,8,64]{2,0,1:T(8,128)(2,1)S(1)}, u32[]{:S(2)}) copy-start(bf16[128,8,64]{2,0,1:T(8,128)(2,1)S(1)} %get-tuple-element.58) | copy-start | bytes 393220
  53.1 5.2 %copy-start.4 = (bf16[128,256]{1,0:T(8,128)(2,1)S(1)}, bf16[128,256]{1,0:T(8,128)(2,1)}, u32[]{:S(2)}) copy-start(bf16[128,256]{1,0:T(8,128)(2,1)} %param.10) | copy-start | bytes 196612
  54.7 9.8 %all-to-all-start = ((bf16[4,32,256]{2,1,0:T(8,128)(2,1)}), bf16[4,32,256]{2,1,0:T(8,128)(2,1)S(1)}, u32[]{:S(2)}, u32[]{:S(2)}) async-start(bf16[4,32,256]{2,1,0:T(8,128)(2,1)} %convert_element_type.70), calls=%async_computation | async-start | bytes 131072 | tf_op jit(solution)/shard_map/all_to_all | solution.py:147
  59.1 12.5 %collective-permute-start.1 = (bf16[64,256]{1,0:T(8,128)(2,1)}, bf16[64,256]{1,0:T(8,128)(2,1)}, u32[]{:S(2)}, u32[]{:S(2)}) collective-permute-start(bf16[64,256]{1,0:T(8,128)(2,1)} %collective-permute-done), channel_id=1, source_target_pairs={{0,4},{4,8},{8,12},{12,16},{16,20},{20,24},{24,28},{28,0},{1,5},{5... | collective-permute-start | bytes 98312 | tf_op jit(solution)/shard_map/ppermute | solution.py:18
  59.1 19.4 %collective-permute-start.5 = (bf16[64,256]{1,0:T(8,128)(2,1)}, bf16[64,256]{1,0:T(8,128)(2,1)}, u32[]{:S(2)}, u32[]{:S(2)}) collective-permute-start(bf16[64,256]{1,0:T(8,128)(2,1)} %collective-permute-done.4), channel_id=1, source_target_pairs={{0,28},{4,0},{8,4},{12,8},{16,12},{20,16},{24,20},{28,24},{1,29},{... | collective-permute-start | bytes 98312 | tf_op jit(solution)/shard_map/ppermute | solution.py:20
  66.5 3.9 %copy-start.3 = (bf16[128,256]{0,1:T(8,128)(2,1)S(1)}, bf16[128,256]{0,1:T(8,128)(2,1)}, u32[]{:S(2)}) copy-start(bf16[128,256]{0,1:T(8,128)(2,1)} %copy.124) | copy-start | bytes 196612
  68.4 18.2 %copy-start.5 = (bf16[64,256]{1,0:T(8,128)(2,1)S(1)}, bf16[64,256]{1,0:T(8,128)(2,1)}, u32[]{:S(2)}) copy-start(bf16[64,256]{1,0:T(8,128)(2,1)} %param.12) | copy-start | bytes 98308
  69.3 9.1 %copy-start.6 = (f32[128,2,4]{0,2,1:T(4,128)S(1)}, f32[128,2,4]{0,2,1:T(4,128)}, u32[]{:S(2)}) copy-start(f32[128,2,4]{0,2,1:T(4,128)} %fusion.2) | copy-start | bytes 12292
  71.5 19.8 %copy-start.1 = (f32[128,2,4,128]{0,3,2,1:T(8,128)S(1)}, f32[128,2,4,128]{0,3,2,1:T(8,128)}, u32[]{:S(2)}) copy-start(f32[128,2,4,128]{0,3,2,1:T(8,128)} %convolution_bitcast_fusion.1) | copy-start | bytes 1572868
  71.6 6.9 %collective-permute-start.2 = (bf16[64,256]{1,0:T(8,128)(2,1)}, bf16[64,256]{1,0:T(8,128)(2,1)S(1)}, u32[]{:S(2)}, u32[]{:S(2)}) collective-permute-start(bf16[64,256]{1,0:T(8,128)(2,1)} %collective-permute-done.1), channel_id=1, source_target_pairs={{0,4},{4,8},{8,12},{12,16},{16,20},{20,24},{24,28},{28,0},{1,5},{5... | collective-permute-start | bytes 98312 | tf_op jit(solution)/shard_map/ppermute | solution.py:18
  78.4 6.6 %collective-permute-start.3 = (bf16[64,256]{1,0:T(8,128)(2,1)S(1)}, bf16[64,256]{1,0:T(8,128)(2,1)S(1)}, u32[]{:S(2)}, u32[]{:S(2)}) collective-permute-start(bf16[64,256]{1,0:T(8,128)(2,1)S(1)} %collective-permute-done.2), channel_id=1, source_target_pairs={{0,4},{4,8},{8,12},{12,16},{16,20},{20,24},{24,28},{28,0},{1,5},{5... | collective-permute-start | bytes 98312 | tf_op jit(solution)/shard_map/ppermute | solution.py:18
  78.5 9.6 %collective-permute-start.6 = (bf16[64,256]{1,0:T(8,128)(2,1)}, bf16[64,256]{1,0:T(8,128)(2,1)S(1)}, u32[]{:S(2)}, u32[]{:S(2)}) collective-permute-start(bf16[64,256]{1,0:T(8,128)(2,1)} %collective-permute-done.5), channel_id=1, source_target_pairs={{0,28},{4,0},{8,4},{12,8},{16,12},{20,16},{24,20},{28,24},{1,29},{... | collective-permute-start | bytes 98312 | tf_op jit(solution)/shard_map/ppermute | solution.py:20
